TPU v7x, 32 devices: a whole 2x2x4 slice. The times are simulated.
32 devices in a mesh: section: 2 (over core), fsdp: 2 (over y), expert: 8 (over z, x).
Axes of the slice: x: 2, y: 2, z: 4, core: 2. Of those that a mesh axis runs over, the one named last changes fastest.
Arguments:
- tokens: bfloat16 [2048, 2048], P(('fsdp', 'expert')), may hold values from -40 to 40
- norm_gain: float32 [2, 2048], P('section'), may hold values from 0.5 to 1.5
- router: bfloat16 [2, 2048, 32], P('section'), may hold values from -0.3125 to 0.3125
- w_gate: bfloat16 [2, 32, 2048, 768], P('section', 'expert', 'fsdp'), may hold values from -0.125 to 0.125
- w_up: bfloat16 [2, 32, 2048, 768], P('section', 'expert', 'fsdp'), may hold values from -0.125 to 0.125
- w_down: bfloat16 [2, 32, 768, 2048], P('section', 'expert', None, 'fsdp'), may hold values from -0.21875 to 0.21875
- routes: int32 [2, 2048, 6], P('section', ('fsdp', 'expert')), may hold values from 0 to 31, all different within a row; in each aligned block of 64 rows (0 to 63, 64 to 127, ..., all dimensions but the last counted through in order) at most 14 rows name the same one
Outputs:
- final_out: bfloat16 [2048, 2048], P(('fsdp', 'expert'), 'section')
- layer_stats: float32 [2], P('section')
Inputs may be any that keep to these rules, and one draw needn't show every extreme that they name: `routes`: each row names 6 different experts; in every aligned block of 64 rows of one layer no expert is named by more than 14 rows, a bound that some block reaches.
All inputs are finite; a program needn't handle non-finite values.
Results may differ from a plain program's by a relative error of at most 0.0065.
Values may be sent and summed in bfloat16 or wider, within the bound.
No kernel may reach another device: no remote copies, remote signals or barrier semaphores. Data moves between devices by JAX's collectives and lax.ppermute only.
A program may use at most 192 MiB of HBM per device.

v0:
```python
import jax
import jax.numpy as jnp
from jax import lax
from jax.sharding import PartitionSpec as P

TOP = 6
BLOCK = 64
epsilon = 1e-06


def other_section(value):
    return lax.ppermute(value, "section", [(0, 1), (1, 0)])


def ring_pairs(count, shift):
    return [(source, (source + shift) % count) for source in range(count)]


def rms_scaled(hidden_rows, gain_row):
    values = hidden_rows.astype(jnp.float32)
    scale = lax.rsqrt(jnp.mean(values * values, axis=-1, keepdims=True) + epsilon)
    return (values * scale * gain_row).astype(jnp.bfloat16)


def gate_weights(normed, router_weight, route_rows):
    logits = jnp.dot(normed, router_weight, preferred_element_type=jnp.float32)
    scores = jax.nn.sigmoid(logits)
    expert_ids = jnp.arange(router_weight.shape[1], dtype=jnp.int32)
    chosen_mask = (route_rows[:, :, None] == expert_ids[None, None, :]).astype(jnp.float32)
    chosen = jnp.sum(scores[:, None, :] * chosen_mask, axis=2)
    return chosen / jnp.sum(chosen, axis=1, keepdims=True)


def slot_positions(route_rows, experts_count, capacity):
    flat_routes = route_rows.reshape(-1)
    onehot = (flat_routes[:, None] == jnp.arange(experts_count, dtype=jnp.int32)[None, :]).astype(
        jnp.int32
    )
    count = flat_routes.shape[0]
    earlier = (jnp.arange(count)[:, None] > jnp.arange(count)[None, :]).astype(jnp.bfloat16)
    before = jnp.dot(
        earlier, onehot.astype(jnp.bfloat16), preferred_element_type=jnp.float32
    ).astype(jnp.int32)
    slot_index = jnp.sum(before * onehot, axis=1)
    return (flat_routes * capacity + slot_index).reshape(route_rows.shape)


def other_half(value):
    return lax.ppermute(value, "zhalf", [(0, 1), (1, 0)])


def half_buffer(positions, normed, slot_ids, fsdp_count, chunk):
    placing = jnp.any(positions[:, :, None] == slot_ids[None, None, :], axis=1).astype(jnp.bfloat16)
    return jnp.einsum(
        "rs,rfd->fsd",
        placing,
        normed.reshape(normed.shape[0], fsdp_count, chunk),
        preferred_element_type=jnp.float32,
    ).astype(jnp.bfloat16)


def expert_layer(entering, route_rows, partner_routes, gain_row, router_weight, weights, capacity):
    gate_w, up_w, down_w = weights
    rows, width = entering.shape
    experts_count = router_weight.shape[1]
    local_experts, chunk, hidden_units = gate_w.shape
    fsdp_count = lax.axis_size("fsdp")
    halves = lax.axis_size("zhalf")
    inner_devices = lax.axis_size("inner")
    half_index = lax.axis_index("zhalf")
    fsdp_index = lax.axis_index("fsdp")
    partner_entering = other_half(entering)
    normed = rms_scaled(entering, gain_row)
    partner_normed = rms_scaled(partner_entering, gain_row)
    mix_weights = gate_weights(normed, router_weight, route_rows)
    positions = slot_positions(route_rows, experts_count, capacity)
    partner_positions = slot_positions(partner_routes, experts_count, capacity)
    half_slots = experts_count // halves * capacity
    local_ids = half_index * half_slots + jnp.arange(half_slots, dtype=jnp.int32)
    first_half = half_index == 0
    lower_normed = jnp.where(first_half, normed, partner_normed)
    upper_normed = jnp.where(first_half, partner_normed, normed)
    lower_positions = jnp.where(first_half, positions, partner_positions)
    upper_positions = jnp.where(first_half, partner_positions, positions)
    group_slots = local_experts * capacity
    both_positions = jnp.stack([lower_positions, upper_positions])
    placing = jnp.any(
        both_positions[:, :, :, None] == local_ids[None, None, None, :], axis=2
    ).astype(jnp.bfloat16)
    placing = placing.reshape(halves, rows, inner_devices, local_experts, capacity)
    both_normed = jnp.stack([lower_normed, upper_normed]).reshape(halves, rows, fsdp_count, chunk)
    outgoing = (
        jnp.einsum("prijc,prfd->fijpcd", placing, both_normed, preferred_element_type=jnp.float32)
        .astype(jnp.bfloat16)
        .reshape(fsdp_count * inner_devices, local_experts, halves * capacity, chunk)
    )
    arrived = lax.all_to_all(outgoing, ("fsdp", "inner"), 0, 2, tiled=True)
    sources = fsdp_count * inner_devices * halves
    arrived_blocks = arrived.reshape(local_experts, fsdp_count, -1, chunk)

    def gate_and_up(rows_in):
        gate_part = jnp.einsum("jrd,jdh->jrh", rows_in, gate_w, preferred_element_type=jnp.float32)
        up_part = jnp.einsum("jrd,jdh->jrh", rows_in, up_w, preferred_element_type=jnp.float32)
        return (gate_part, up_part)

    received = []
    for shift in range(1, fsdp_count):
        target = (fsdp_index + shift) % fsdp_count
        outgoing_pair = jnp.stack(
            gate_and_up(lax.dynamic_index_in_dim(arrived_blocks, target, 1, keepdims=False))
        ).astype(jnp.bfloat16)
        received.append(lax.ppermute(outgoing_pair, "fsdp", ring_pairs(fsdp_count, shift)))
    gate_sum, up_sum = gate_and_up(
        lax.dynamic_index_in_dim(arrived_blocks, fsdp_index, 1, keepdims=False)
    )
    for got in received:
        gate_sum = gate_sum + got[0].astype(jnp.float32)
        up_sum = up_sum + got[1].astype(jnp.float32)
    inner_act = (jax.nn.silu(gate_sum) * up_sum).astype(jnp.bfloat16)
    inner_pieces = [inner_act]
    for shift in range(1, fsdp_count):
        inner_pieces.append(lax.ppermute(inner_act, "fsdp", ring_pairs(fsdp_count, shift)))
    order = (fsdp_index - jnp.arange(fsdp_count, dtype=jnp.int32)) % fsdp_count
    inner_all = jnp.take(jnp.stack(inner_pieces), order, axis=0).reshape(
        fsdp_count, local_experts, inner_devices, halves, capacity, hidden_units
    )
    sending = jnp.einsum(
        "fjipch,jhd->fpijcd", inner_all, down_w, preferred_element_type=jnp.float32
    ).astype(jnp.bfloat16)
    returned = lax.all_to_all(
        sending.reshape(sources, group_slots, chunk), ("fsdp", "zhalf", "inner"), 0, 0, tiled=True
    )
    slot_ids = jnp.arange(experts_count * capacity, dtype=jnp.int32)
    hits = positions[:, :, None] == slot_ids[None, None, :]
    combining = jnp.sum(jnp.where(hits, mix_weights[:, :, None], 0.0), axis=1)
    branch_sum = jnp.einsum(
        "rs,fsd->rfd",
        combining,
        returned.reshape(fsdp_count, experts_count * capacity, chunk).astype(jnp.float32),
        precision=lax.Precision.HIGHEST,
        preferred_element_type=jnp.float32,
    ).reshape(rows, width)
    return (entering.astype(jnp.float32) + branch_sum).astype(jnp.bfloat16)


def body(tokens, norm_gain, router, w_gate, w_up, w_down, routes):
    section_index = lax.axis_index("section")
    sections = lax.axis_size("section")
    token_rows, width = tokens.shape
    piece = token_rows // sections
    experts_count = router.shape[2]
    block_capacity = (7 * BLOCK * TOP + 6 * experts_count - 1) // (6 * experts_count)
    capacity = block_capacity * (piece // BLOCK)
    own_weights = (w_gate[0], w_up[0], w_down[0])
    other_weights = tuple((other_section(w) for w in own_weights))
    own_small = (norm_gain[0], router[0])
    packed = jnp.concatenate([own_small[0][:, None], own_small[1].astype(jnp.float32)], axis=1)
    other_packed = other_section(packed)
    other_small = (other_packed[:, 0], other_packed[:, 1:].astype(router.dtype))
    own_routes = routes[0]
    section_routes = other_section(own_routes)
    half_routes = other_half(own_routes)
    diagonal_routes = lax.ppermute(
        own_routes, ("section", "zhalf"), [(0, 3), (3, 0), (1, 2), (2, 1)]
    )
    hidden = lax.dynamic_slice_in_dim(tokens, section_index * piece, piece, 0)
    squares = []
    for layer in range(sections):
        mine = section_index == layer
        gain_row, router_weight = [jnp.where(mine, a, b) for a, b in zip(own_small, other_small)]
        weights = tuple((jnp.where(mine, a, b) for a, b in zip(own_weights, other_weights)))
        route_all = jnp.where(mine, own_routes, section_routes)
        partner_all = jnp.where(mine, half_routes, diagonal_routes)
        route_rows = lax.dynamic_slice_in_dim(route_all, section_index * piece, piece, 0)
        partner_rows = lax.dynamic_slice_in_dim(partner_all, section_index * piece, piece, 0)
        hidden = expert_layer(
            hidden, route_rows, partner_rows, gain_row, router_weight, weights, capacity
        )
        values = hidden.astype(jnp.float32)
        squares.append(jnp.sum(values * values))
    everyone = ("section", "fsdp", "zhalf", "inner")
    expert_devices = lax.axis_size("zhalf") * lax.axis_size("inner")
    device_count = sections * lax.axis_size("fsdp") * expert_devices
    square_rows = jnp.broadcast_to(jnp.stack(squares)[None, :], (device_count, sections))
    totals = jnp.sum(lax.all_to_all(square_rows, everyone, 0, 0, tiled=True), axis=0)
    token_total = token_rows * lax.axis_size("fsdp") * expert_devices
    stats = jnp.sqrt(totals / (token_total * width))
    layer_stats = lax.dynamic_slice_in_dim(stats, section_index, 1, 0)
    half_width = width // 2
    keep = lax.dynamic_slice_in_dim(hidden, section_index * half_width, half_width, 1)
    send = lax.dynamic_slice_in_dim(hidden, (1 - section_index) * half_width, half_width, 1)
    arrived = other_section(send)
    final_out = jnp.where(
        section_index == 0,
        jnp.concatenate([keep, arrived], axis=0),
        jnp.concatenate([arrived, keep], axis=0),
    )
    return (final_out, layer_stats)


def solution(mesh):
    sizes = dict(zip(mesh.axis_names, mesh.devices.shape))
    devices = mesh.devices.reshape(sizes["section"], sizes["fsdp"], 2, sizes["expert"] // 2)
    split_mesh = jax.sharding.Mesh(devices, ("section", "fsdp", "zhalf", "inner"))
    tokens_axes = ("fsdp", "zhalf", "inner")
    experts_axes = ("zhalf", "inner")
    in_specs = (
        P(tokens_axes, None),
        P("section", None),
        P("section", None, None),
        P("section", experts_axes, "fsdp", None),
        P("section", experts_axes, "fsdp", None),
        P("section", experts_axes, None, "fsdp"),
        P("section", tokens_axes, None),
    )
    out_specs = (P(tokens_axes, "section"), P("section"))
    return jax.shard_map(
        body, mesh=split_mesh, in_specs=in_specs, out_specs=out_specs, check_vma=False
    )
```

profile of v0, /device:TPU:0, one launch (start us, length us, event | category | flops | bytes accessed | tf_op | source)
XLA Modules:
  0.0 329.2 jit_solution(16897650569379515647)
XLA Ops:
  0.6 0.8 copy.121
  1.4 4.1 %collective-permute-start.4 = (s32[128,6]{1,0:T(8,128)S(1)}, s32[128,6]{1,0:T(8,128)S(1)}, u32[]{:S(2)}, u32[]{:S(2)}) collective-permute-start(s32[128,6]{1,0:T(8,128)S(1)} %bitcast.209), channel_id=1, source_target_pairs={{0,4},{4,0},{1,5},{5,1},{2,6},{6,2},{3,7},{7,3},{8,12},{12,8},{9,1... | collective-permute-start | bytes 9224 | tf_op jit(solution)/shard_map/ppermute | solution.py:49
  5.7 1.1 fusion.78
  6.8 2.9 collective-permute-start.3
  9.8 0.9 bitcast_convert_fusion
  10.7 0.8 pad_maximum_fusion.4
  11.6 0.5 collective-permute-start.6
  12.1 5.7 %collective-permute-done.5 = s32[128,6]{1,0:T(8,128)S(1)} collective-permute-done((s32[128,6]{1,0:T(8,128)S(1)}, s32[128,6]{1,0:T(8,128)S(1)}, u32[]{:S(2)}, u32[]{:S(2)}) %collective-permute-start.5) | collective-permute-done | bytes 3104 | tf_op jit(solution)/shard_map/ppermute | solution.py:163
  18.0 0.2 fusion.41
  18.4 0.2 fusion.43
  20.2 0.3 compare_reduce_fusion
  20.7 2.3 collective-permute-done.3
  23.2 0.2 broadcast_select_fusion.45
  23.9 0.7 convert_bitcast_fusion.3
  24.6 2.8 copy.128
  27.4 4.1 %all-to-all-start = ((bf16[8,4,28,1024]{3,1,2,0:T(4,128)(2,1)}), bf16[8,4,28,1024]{3,1,2,0:T(4,128)(2,1)S(1)}, u32[]{:S(2)}, u32[]{:S(2)}) async-start(bf16[8,4,28,1024]{3,1,2,0:T(4,128)(2,1)} %bitcast.198), calls=%async_computation | async-start | bytes 3670016 | tf_op jit(solution)/shard_map/all_to_all | solution.py:97
  31.6 29.0 %all-to-all-done = bf16[8,4,28,1024]{3,1,2,0:T(4,128)(2,1)S(1)} async-done(((bf16[8,4,28,1024]{3,1,2,0:T(4,128)(2,1)}), bf16[8,4,28,1024]{3,1,2,0:T(4,128)(2,1)S(1)}, u32[]{:S(2)}, u32[]{:S(2)}) %all-to-all-start) | async-done | bytes 1835040 | tf_op jit(solution)/shard_map/all_to_all | solution.py:97
  60.6 0.6 constant_dynamic-slice_fusion.4
  61.2 4.8 %fusion.32 = bf16[1,4,112,768]{3,2,1,0:T(8,128)(2,1)S(1)} fusion(bf16[4,1024,768]{2,1,0:T(8,128)(2,1)} %collective-permute-done.6, pred[]{:T(512)S(6)} %eq.78, bf16[4,1,112,1024]{3,0,2,1:T(4,128)(2,1)S(1)} %get-tuple-element.19, bf16[1,4,1024,768]{3,2,1,0:T(8,128)(2,1)} %param.12), kind=kOutput, calls=%fused_computation.48 | convolution fusion | flops 708132864 | bytes 14188545 | tf_op jit(solution)/shard_map/jrd,jdh->jrh/dot_general | solution.py:102
  66.1 1.8 fusion.33
  68.1 0.6 collective-permute-start.8
  68.7 30.0 %collective-permute-done.8 = bf16[2,4,112,768]{3,2,1,0:T(8,128)(2,1)S(1)} collective-permute-done((bf16[2,4,112,768]{3,2,1,0:T(8,128)(2,1)S(1)}, bf16[2,4,112,768]{3,2,1,0:T(8,128)(2,1)S(1)}, u32[]{:S(2)}, u32[]{:S(2)}) %collective-permute-start.8) | collective-permute-done | bytes 1376288 | tf_op jit(solution)/shard_map/ppermute | solution.py:112
  98.8 1.9 fusion.27
  100.6 2.0 multiply_convert_fusion.1
  102.7 0.6 collective-permute-start.9
  103.4 10.8 %collective-permute-done.9 = bf16[4,112,768]{2,1,0:T(8,128)(2,1)S(1)} collective-permute-done((bf16[4,112,768]{2,1,0:T(8,128)(2,1)S(1)}, bf16[4,112,768]{2,1,0:T(8,128)(2,1)S(1)}, u32[]{:S(2)}, u32[]{:S(2)}) %collective-permute-start.9) | collective-permute-done | bytes 688160 | tf_op jit(solution)/shard_map/ppermute | solution.py:122
  114.3 0.6 gather_fusion
  115.2 0.7 copy.131
  115.9 4.7 %convert_bitcast_fusion.2 = bf16[2,2,4,4,14,1024]{5,4,1,2,0,3:T(8,128)(2,1)S(1)} fusion(bf16[4,768,1024]{2,1,0:T(8,128)(2,1)} %collective-permute-done.2, pred[]{:T(512)S(6)} %eq.78, bf16[2,4,4,2,14,768]{5,1,4,3,2,0:T(4,128)(2,1)S(1)} %bitcast.203, bf16[1,4,768,1024]{3,2,1,0:T(8,128)(2,1)} %param.14), kind=kOutput, calls=%fused_computation.28 | convolution fusion | flops 1413349376 | bytes 15794177 | tf_op jit(solution)/shard_map/fjipch,jhd->fpijcd/dot_general | solution.py:127
  120.8 1.5 reshape.228
  122.3 4.5 %all-to-all-start.1 = ((bf16[16,56,1024]{2,1,0:T(8,128)(2,1)}), bf16[16,56,1024]{2,1,0:T(8,128)(2,1)S(1)}, u32[]{:S(2)}, u32[]{:S(2)}) async-start(bf16[16,56,1024]{2,1,0:T(8,128)(2,1)} %reshape.228), calls=%async_computation.1 | async-start | bytes 3670016 | tf_op jit(solution)/shard_map/all_to_all | solution.py:130
  127.0 0.3 fusion.49
  127.5 39.0 %all-to-all-done.1 = bf16[16,56,1024]{2,1,0:T(8,128)(2,1)S(1)} async-done(((bf16[16,56,1024]{2,1,0:T(8,128)(2,1)}), bf16[16,56,1024]{2,1,0:T(8,128)(2,1)S(1)}, u32[]{:S(2)}, u32[]{:S(2)}) %all-to-all-start.1) | async-done | bytes 1835040 | tf_op jit(solution)/shard_map/all_to_all | solution.py:130
  166.6 1.7 fusion.70
  168.3 2.0 collective-permute-start.10
  170.5 10.9 %collective-permute-done.10 = bf16[64,2048]{1,0:T(8,128)(2,1)S(1)} collective-permute-done((bf16[64,2048]{1,0:T(8,128)(2,1)S(1)}, bf16[64,2048]{1,0:T(8,128)(2,1)S(1)}, u32[]{:S(2)}, u32[]{:S(2)}) %collective-permute-start.10) | collective-permute-done | bytes 262176 | tf_op jit(solution)/shard_map/ppermute | solution.py:49
  181.6 0.2 broadcast_select_fusion.43
  182.4 0.7 convert_bitcast_fusion.1
  183.1 1.6 copy.142
  184.6 28.3 %all_to_all.46 = bf16[8,4,28,1024]{3,1,2,0:T(4,128)(2,1)S(1)} all-to-all(bf16[8,4,28,1024]{3,1,2,0:T(4,128)(2,1)S(1)} %bitcast.202), channel_id=1, replica_groups=mesh['section'=2,'fsdp'=2,'zhalf'=2,'inner'=4] {'fsdp','inner'}, dimensions={0} | all-to-all | bytes 3670016 | tf_op jit(solution)/shard_map/all_to_all | solution.py:97
  212.9 0.6 constant_dynamic-slice_fusion.2
  213.6 4.8 %fusion.34 = bf16[1,4,112,768]{3,2,1,0:T(8,128)(2,1)S(1)} fusion(bf16[4,1024,768]{2,1,0:T(8,128)(2,1)} %collective-permute-done.6, pred[]{:T(512)S(6)} %eq.172, bf16[4,1,112,1024]{3,0,2,1:T(4,128)(2,1)S(1)} %get-tuple-element.17, bf16[1,4,1024,768]{3,2,1,0:T(8,128)(2,1)S(1)} %bitcast.222), kind=kOutput, calls=%fused_computation.50 | convolution fusion | flops 708132864 | bytes 14188545 | tf_op jit(solution)/shard_map/jrd,jdh->jrh/dot_general | solution.py:102
  218.4 4.7 %fusion.35 = bf16[1,4,112,768]{3,2,1,0:T(8,128)(2,1)S(1)} fusion(bf16[4,1024,768]{2,1,0:T(8,128)(2,1)} %collective-permute-done.7, pred[]{:T(512)S(6)} %eq.172, bf16[4,1,112,1024]{3,0,2,1:T(4,128)(2,1)S(1)} %get-tuple-element.17, bf16[1,4,1024,768]{3,2,1,0:T(8,128)(2,1)S(1)} %bitcast.227), kind=kOutput, calls=%fused_computation.51 | convolution fusion | flops 708132864 | bytes 14188545 | tf_op jit(solution)/shard_map/jrd,jdh->jrh/dot_general | solution.py:103
  223.3 0.6 collective-permute-start.11
  223.9 26.6 %collective-permute-done.11 = bf16[2,4,112,768]{3,2,1,0:T(8,128)(2,1)S(1)} collective-permute-done((bf16[2,4,112,768]{3,2,1,0:T(8,128)(2,1)S(1)}, bf16[2,4,112,768]{3,2,1,0:T(8,128)(2,1)S(1)}, u32[]{:S(2)}, u32[]{:S(2)}) %collective-permute-start.11) | collective-permute-done | bytes 1376288 | tf_op jit(solution)/shard_map/ppermute | solution.py:112
  250.5 4.7 %fusion.25 = f32[4,112,768]{2,1,0:T(8,128)S(1)} fusion(bf16[4,1024,768]{2,1,0:T(8,128)(2,1)} %collective-permute-done.6, pred[]{:T(512)S(6)} %eq.172, bf16[4,1,112,1024]{3,0,2,1:T(4,128)(2,1)S(1)} %get-tuple-element.18, bf16[2,4,112,768]{3,2,1,0:T(8,128)(2,1)S(1)} %collective-permute-done.11, bf16[1,4,1024,768]{3,2,1,0:T(8,128)(2,1)S(1)} %bitcast.222), kind=kOutput, calls=%fused_computation.33 | convolution fusion | flops 708476928 | bytes 15564801 | tf_op jit(solution)/shard_map/jrd,jdh->jrh/dot_general | solution.py:102
  255.2 4.9 %multiply_convert_fusion = bf16[4,112,768]{2,1,0:T(8,128)(2,1)S(1)} fusion(f32[4,112,768]{2,1,0:T(8,128)S(1)} %fusion.25, bf16[4,1024,768]{2,1,0:T(8,128)(2,1)} %collective-permute-done.7, pred[]{:T(512)S(6)} %eq.172, bf16[4,1,112,1024]{3,0,2,1:T(4,128)(2,1)S(1)} %get-tuple-element.18, bf16[2,4,112,768]{3,2,1,0:T(8,128)(2,1)S(1)} %collective-permute-done.11, ...), kind=kOutput, calls=%fused_computation.40 | convolution fusion | flops 710541312 | bytes 16252929 | tf_op jit(solution)/shard_map/jrd,jdh->jrh/dot_general | solution.py:103
  260.2 0.6 collective-permute-start.12
  260.8 10.4 %collective-permute-done.12 = bf16[4,112,768]{2,1,0:T(8,128)(2,1)S(1)} collective-permute-done((bf16[4,112,768]{2,1,0:T(8,128)(2,1)S(1)}, bf16[4,112,768]{2,1,0:T(8,128)(2,1)S(1)}, u32[]{:S(2)}, u32[]{:S(2)}) %collective-permute-start.12) | collective-permute-done | bytes 688160 | tf_op jit(solution)/shard_map/ppermute | solution.py:122
  271.3 0.6 gather_fusion.1
  272.1 0.7 copy.145
  272.9 6.5 %convert_bitcast_fusion = bf16[2,2,4,4,14,1024]{5,4,1,2,0,3:T(8,128)(2,1)S(1)} fusion(bf16[4,768,1024]{2,1,0:T(8,128)(2,1)} %collective-permute-done.2, pred[]{:T(512)S(6)} %eq.172, bf16[2,4,4,2,14,768]{5,1,4,3,2,0:T(4,128)(2,1)S(1)} %bitcast.204, bf16[1,4,768,1024]{3,2,1,0:T(8,128)(2,1)} %param.14), kind=kOutput, calls=%fused_computation.26 | convolution fusion | flops 1413349376 | bytes 15794177 | tf_op jit(solution)/shard_map/fjipch,jhd->fpijcd/dot_general | solution.py:127
  279.6 1.5 reshape.230
  281.1 4.3 %all-to-all-start.3 = ((bf16[16,56,1024]{2,1,0:T(8,128)(2,1)}), bf16[16,56,1024]{2,1,0:T(8,128)(2,1)S(1)}, u32[]{:S(2)}, u32[]{:S(2)}) async-start(bf16[16,56,1024]{2,1,0:T(8,128)(2,1)} %reshape.230), calls=%async_computation.3 | async-start | bytes 3670016 | tf_op jit(solution)/shard_map/all_to_all | solution.py:130
  285.6 0.3 fusion.46
  286.2 27.6 %all-to-all-done.3 = bf16[16,56,1024]{2,1,0:T(8,128)(2,1)S(1)} async-done(((bf16[16,56,1024]{2,1,0:T(8,128)(2,1)}), bf16[16,56,1024]{2,1,0:T(8,128)(2,1)S(1)}, u32[]{:S(2)}, u32[]{:S(2)}) %all-to-all-start.3) | async-done | bytes 1835040 | tf_op jit(solution)/shard_map/all_to_all | solution.py:130
  313.9 1.7 multiply_reduce_fusion
  315.6 1.4 pad_maximum_fusion.5
  317.0 0.6 broadcast_in_dim.32
  317.6 3.1 all-to-all-start.4
  320.7 0.3 collective-permute-start.13
  321.1 6.7 %all-to-all-done.4 = f32[32,1,2]{2,1,0:T(1,128)S(1)} async-done(((f32[32,1,2]{2,1,0:T(1,128)}), f32[32,1,2]{2,1,0:T(1,128)S(1)}, u32[]{:S(2)}, u32[]{:S(2)}) %all-to-all-start.4) | async-done | bytes 288 | tf_op jit(solution)/shard_map/all_to_all | solution.py:185
  327.9 0.6 dynamic_slice.48
  328.5 0.8 maximum_select_fusion
  (107 shorter events, 6.2 us)
Async XLA Ops:
  1.4 10.2 %collective-permute-start.4 = (s32[128,6]{1,0:T(8,128)S(1)}, s32[128,6]{1,0:T(8,128)S(1)}, u32[]{:S(2)}, u32[]{:S(2)}) collective-permute-start(s32[128,6]{1,0:T(8,128)S(1)} %bitcast.209), channel_id=1, source_target_pairs={{0,4},{4,0},{1,5},{5,1},{2,6},{6,2},{3,7},{7,3},{8,12},{12,8},{9,1... | collective-permute-start | bytes 9224 | tf_op jit(solution)/shard_map/ppermute | solution.py:49
  5.5 12.3 %collective-permute-start.5 = (s32[128,6]{1,0:T(8,128)S(1)}, s32[128,6]{1,0:T(8,128)S(1)}, u32[]{:S(2)}, u32[]{:S(2)}) collective-permute-start(s32[128,6]{1,0:T(8,128)S(1)} %bitcast.210), channel_id=1, source_target_pairs={{0,20},{20,0},{4,16},{16,4},{1,21},{21,1},{5,17},{17,5},{2,22},{22... | collective-permute-start | bytes 9224 | tf_op jit(solution)/shard_map/ppermute | solution.py:163
  5.5 13.3 %collective-permute-start = (s32[128,6]{1,0:T(8,128)S(1)}, s32[128,6]{1,0:T(8,128)S(1)}, u32[]{:S(2)}, u32[]{:S(2)}) collective-permute-start(s32[128,6]{1,0:T(8,128)S(1)} %bitcast.211), channel_id=1, source_target_pairs={{0,16},{16,0},{1,17},{17,1},{2,18},{18,2},{3,19},{19,3},{4,20},{20... | collective-permute-start | bytes 9224 | tf_op jit(solution)/shard_map/ppermute | solution.py:12
  6.8 16.2 %collective-permute-start.3 = (bf16[64,2048]{1,0:T(8,128)(2,1)S(1)}, bf16[64,2048]{1,0:T(8,128)(2,1)S(1)}, u32[]{:S(2)}, u32[]{:S(2)}) collective-permute-start(bf16[64,2048]{1,0:T(8,128)(2,1)S(1)} %get-tuple-element.16), channel_id=1, source_target_pairs={{0,4},{4,0},{1,5},{5,1},{2,6},{6,2},{3,7},{7,3},{8,12},{12,8},{9,1... | collective-permute-start | bytes 786440 | tf_op jit(solution)/shard_map/ppermute | solution.py:49
  10.7 12.5 %copy-start.1 = (f32[1,2048]{1,0:T(1,128)S(1)}, f32[1,2048]{1,0:T(1,128)}, u32[]{:S(2)}) copy-start(f32[1,2048]{1,0:T(1,128)} %param.10) | copy-start | bytes 24580
  11.5 11.7 %collective-permute-start.1 = (f32[2048,33]{0,1:T(8,128)S(1)}, f32[2048,33]{0,1:T(8,128)S(1)}, u32[]{:S(2)}, u32[]{:S(2)}) collective-permute-start(f32[2048,33]{0,1:T(8,128)S(1)} %pad_maximum_fusion.4), channel_id=1, source_target_pairs={{0,16},{16,0},{1,17},{17,1},{2,18},{18,2},{3,19},{19,3},{4,20},{20... | collective-permute-start | bytes 811016 | tf_op jit(solution)/shard_map/ppermute | solution.py:12
  11.6 49.6 %collective-permute-start.6 = (bf16[4,1024,768]{2,1,0:T(8,128)(2,1)}, bf16[4,1024,768]{2,1,0:T(8,128)(2,1)}, u32[]{:S(2)}, u32[]{:S(2)}) collective-permute-start(bf16[4,1024,768]{2,1,0:T(8,128)(2,1)} %bitcast.218), channel_id=1, source_target_pairs={{0,16},{16,0},{1,17},{17,1},{2,18},{18,2},{3,19},{19,3},{4,20},{20... | collective-permute-start | bytes 18874376 | tf_op jit(solution)/shard_map/ppermute | solution.py:12
  17.9 48.2 %collective-permute-start.7 = (bf16[4,1024,768]{2,1,0:T(8,128)(2,1)}, bf16[4,1024,768]{2,1,0:T(8,128)(2,1)}, u32[]{:S(2)}, u32[]{:S(2)}) collective-permute-start(bf16[4,1024,768]{2,1,0:T(8,128)(2,1)} %bitcast.223), channel_id=1, source_target_pairs={{0,16},{16,0},{1,17},{17,1},{2,18},{18,2},{3,19},{19,3},{4,20},{20... | collective-permute-start | bytes 18874376 | tf_op jit(solution)/shard_map/ppermute | solution.py:12
  23.2 1.4 copy-start.2
  27.4 33.2 %all-to-all-start = ((bf16[8,4,28,1024]{3,1,2,0:T(4,128)(2,1)}), bf16[8,4,28,1024]{3,1,2,0:T(4,128)(2,1)S(1)}, u32[]{:S(2)}, u32[]{:S(2)}) async-start(bf16[8,4,28,1024]{3,1,2,0:T(4,128)(2,1)} %bitcast.198), calls=%async_computation | async-start | bytes 3670016 | tf_op jit(solution)/shard_map/all_to_all | solution.py:97
  31.5 84.4 %collective-permute-start.2 = (bf16[4,768,1024]{2,1,0:T(8,128)(2,1)}, bf16[4,768,1024]{2,1,0:T(8,128)(2,1)}, u32[]{:S(2)}, u32[]{:S(2)}) collective-permute-start(bf16[4,768,1024]{2,1,0:T(8,128)(2,1)} %bitcast.228), channel_id=1, source_target_pairs={{0,16},{16,0},{1,17},{17,1},{2,18},{18,2},{3,19},{19,3},{4,20},{20... | collective-permute-start | bytes 18874376 | tf_op jit(solution)/shard_map/ppermute | solution.py:12
  60.6 5.5 %slice-start.4 = ((s8[6291456]{0:T(1024)(128)(4,1)}), s8[4194304]{0:T(1024)(128)(4,1)S(1)}, s32[]{:S(2)}) async-start(s8[6291456]{0:T(1024)(128)(4,1)} %bitcast.224), calls=%async_computation.9 | async-start | bytes 8388608
  61.2 4.9 %slice-start.5 = ((s8[6291456]{0:T(1024)(128)(4,1)}), s8[2097152]{0:T(1024)(128)(4,1)S(1)}, s32[]{:S(2)}) async-start(s8[6291456]{0:T(1024)(128)(4,1)} %bitcast.224), calls=%async_computation.10 | async-start | bytes 4194304
  61.2 37.5 %slice-start = ((s8[6291456]{0:T(1024)(128)(4,1)}), s8[4194304]{0:T(1024)(128)(4,1)S(1)}, s32[]{:S(2)}) async-start(s8[6291456]{0:T(1024)(128)(4,1)} %bitcast.219), calls=%async_computation.5 | async-start | bytes 8388608
  66.0 32.7 %slice-start.1 = ((s8[6291456]{0:T(1024)(128)(4,1)}), s8[2097152]{0:T(1024)(128)(4,1)S(1)}, s32[]{:S(2)}) async-start(s8[6291456]{0:T(1024)(128)(4,1)} %bitcast.219), calls=%async_computation.6 | async-start | bytes 4194304
  68.1 30.7 %collective-permute-start.8 = (bf16[2,4,112,768]{3,2,1,0:T(8,128)(2,1)S(1)}, bf16[2,4,112,768]{3,2,1,0:T(8,128)(2,1)S(1)}, u32[]{:S(2)}, u32[]{:S(2)}) collective-permute-start(bf16[2,4,112,768]{3,2,1,0:T(8,128)(2,1)S(1)} %pad_maximum_fusion), channel_id=1, source_target_pairs={{0,8},{8,0},{1,9},{9,1},{2,10},{10,2},{3,11},{11,3},{4,12},{12,4},... | collective-permute-start | bytes 4128776 | tf_op jit(solution)/shard_map/ppermute | solution.py:112
  102.7 11.5 %collective-permute-start.9 = (bf16[4,112,768]{2,1,0:T(8,128)(2,1)S(1)}, bf16[4,112,768]{2,1,0:T(8,128)(2,1)S(1)}, u32[]{:S(2)}, u32[]{:S(2)}) collective-permute-start(bf16[4,112,768]{2,1,0:T(8,128)(2,1)S(1)} %multiply_convert_fusion.1), channel_id=1, source_target_pairs={{0,8},{8,0},{1,9},{9,1},{2,10},{10,2},{3,11},{11,3},{4,12},{12,4},... | collective-permute-start | bytes 2064392 | tf_op jit(solution)/shard_map/ppermute | solution.py:122
  122.3 4.6 %copy-start = (bf16[1,2048,32]{1,2,0:T(8,128)(2,1)S(1)}, bf16[1,2048,32]{1,2,0:T(8,128)(2,1)}, u32[]{:S(2)}) copy-start(bf16[1,2048,32]{1,2,0:T(8,128)(2,1)} %param.11) | copy-start | bytes 393220
  122.3 4.6 %copy-start.3 = (f32[2048,33]{0,1:T(8,128)S(1)}, f32[2048,33]{0,1:T(8,128)}, u32[]{:S(2)}) copy-start(f32[2048,33]{0,1:T(8,128)} %copy-done.2) | copy-start | bytes 811012
  122.3 44.2 %all-to-all-start.1 = ((bf16[16,56,1024]{2,1,0:T(8,128)(2,1)}), bf16[16,56,1024]{2,1,0:T(8,128)(2,1)S(1)}, u32[]{:S(2)}, u32[]{:S(2)}) async-start(bf16[16,56,1024]{2,1,0:T(8,128)(2,1)} %reshape.228), calls=%async_computation.1 | async-start | bytes 3670016 | tf_op jit(solution)/shard_map/all_to_all | solution.py:130
  168.3 13.1 %collective-permute-start.10 = (bf16[64,2048]{1,0:T(8,128)(2,1)S(1)}, bf16[64,2048]{1,0:T(8,128)(2,1)S(1)}, u32[]{:S(2)}, u32[]{:S(2)}) collective-permute-start(bf16[64,2048]{1,0:T(8,128)(2,1)S(1)} %get-tuple-element.33), channel_id=1, source_target_pairs={{0,4},{4,0},{1,5},{5,1},{2,6},{6,2},{3,7},{7,3},{8,12},{12,8},{9,1... | collective-permute-start | bytes 786440 | tf_op jit(solution)/shard_map/ppermute | solution.py:49
  181.9 31.7 %slice-start.2 = ((s8[6291456]{0:T(1024)(128)(4,1)}), s8[2097152]{0:T(1024)(128)(4,1)S(1)}, s32[]{:S(2)}) async-start(s8[6291456]{0:T(1024)(128)(4,1)} %bitcast.221), calls=%async_computation.7 | async-start | bytes 4194304
  183.0 30.5 %slice-start.3 = ((s8[6291456]{0:T(1024)(128)(4,1)}), s8[4194304]{0:T(1024)(128)(4,1)S(1)}, s32[]{:S(2)}) async-start(s8[6291456]{0:T(1024)(128)(4,1)} %bitcast.221), calls=%async_computation.8 | async-start | bytes 8388608
  212.9 5.5 %slice-start.6 = ((s8[6291456]{0:T(1024)(128)(4,1)}), s8[4194304]{0:T(1024)(128)(4,1)S(1)}, s32[]{:S(2)}) async-start(s8[6291456]{0:T(1024)(128)(4,1)} %bitcast.226), calls=%async_computation.11 | async-start | bytes 8388608
  213.6 4.8 %slice-start.7 = ((s8[6291456]{0:T(1024)(128)(4,1)}), s8[2097152]{0:T(1024)(128)(4,1)S(1)}, s32[]{:S(2)}) async-start(s8[6291456]{0:T(1024)(128)(4,1)} %bitcast.226), calls=%async_computation.12 | async-start | bytes 4194304
  223.3 27.2 %collective-permute-start.11 = (bf16[2,4,112,768]{3,2,1,0:T(8,128)(2,1)S(1)}, bf16[2,4,112,768]{3,2,1,0:T(8,128)(2,1)S(1)}, u32[]{:S(2)}, u32[]{:S(2)}) collective-permute-start(bf16[2,4,112,768]{3,2,1,0:T(8,128)(2,1)S(1)} %pad_maximum_fusion.2), channel_id=1, source_target_pairs={{0,8},{8,0},{1,9},{9,1},{2,10},{10,2},{3,11},{11,3},{4,12},{12,4},... | collective-permute-start | bytes 4128776 | tf_op jit(solution)/shard_map/ppermute | solution.py:112
  260.2 11.0 %collective-permute-start.12 = (bf16[4,112,768]{2,1,0:T(8,128)(2,1)S(1)}, bf16[4,112,768]{2,1,0:T(8,128)(2,1)S(1)}, u32[]{:S(2)}, u32[]{:S(2)}) collective-permute-start(bf16[4,112,768]{2,1,0:T(8,128)(2,1)S(1)} %multiply_convert_fusion), channel_id=1, source_target_pairs={{0,8},{8,0},{1,9},{9,1},{2,10},{10,2},{3,11},{11,3},{4,12},{12,4},... | collective-permute-start | bytes 2064392 | tf_op jit(solution)/shard_map/ppermute | solution.py:122
  281.1 4.5 %copy-start.4 = (f32[2048,33]{0,1:T(8,128)S(1)}, f32[2048,33]{0,1:T(8,128)}, u32[]{:S(2)}) copy-start(f32[2048,33]{0,1:T(8,128)} %copy-done.2) | copy-start | bytes 811012
  281.1 32.7 %all-to-all-start.3 = ((bf16[16,56,1024]{2,1,0:T(8,128)(2,1)}), bf16[16,56,1024]{2,1,0:T(8,128)(2,1)S(1)}, u32[]{:S(2)}, u32[]{:S(2)}) async-start(bf16[16,56,1024]{2,1,0:T(8,128)(2,1)} %reshape.230), calls=%async_computation.3 | async-start | bytes 3670016 | tf_op jit(solution)/shard_map/all_to_all | solution.py:130
  317.6 10.2 %all-to-all-start.4 = ((f32[32,1,2]{2,1,0:T(1,128)}), f32[32,1,2]{2,1,0:T(1,128)S(1)}, u32[]{:S(2)}, u32[]{:S(2)}) async-start(f32[32,1,2]{2,1,0:T(1,128)} %broadcast_in_dim.32), calls=%async_computation.4 | async-start | bytes 32768 | tf_op jit(solution)/shard_map/all_to_all | solution.py:185
  320.7 7.7 %collective-permute-start.13 = (bf16[64,1024]{1,0:T(8,128)(2,1)S(1)}, bf16[64,1024]{1,0:T(8,128)(2,1)S(1)}, u32[]{:S(2)}, u32[]{:S(2)}) collective-permute-start(bf16[64,1024]{1,0:T(8,128)(2,1)S(1)} %get-tuple-element.28), channel_id=1, source_target_pairs={{0,16},{16,0},{1,17},{17,1},{2,18},{18,2},{3,19},{19,3},{4,20},{20... | collective-permute-start | bytes 393224 | tf_op jit(solution)/shard_map/ppermute | solution.py:12
where the time goes:
time: 330 us; the launch traced here: 329 us
  waiting for transfers between devices  199 us (60%)
  matrix products  47.2 us (14%)
  starting transfers between devices  28.7 us (9%)
  blocking collectives  28.3 us (9%)
  local copies, waits for them, and re-layouts  16.9 us (5%)
  other arithmetic  7.57 us (2%)
    all_to_all x2, waiting for transfers between devices, expert_layer(): lax.all_to_all(sending.reshape(sources, group_slots, chunk), ('fsdp', 'zh...  66.6 us
    ppermute x2, waiting for transfers between devices, expert_layer(): lax.ppermute(outgoing_pair, 'fsdp', ring_pairs(fsdp_count, shift))  56.6 us
    all_to_all x1, waiting for transfers between devices, expert_layer(): arrived = lax.all_to_all(outgoing, ('fsdp', 'inner'), 0, 2, tiled=True)  29 us
    all_to_all x1, blocking collectives, expert_layer(): arrived = lax.all_to_all(outgoing, ('fsdp', 'inner'), 0, 2, tiled=True)  28.3 us
    ppermute x2, waiting for transfers between devices, expert_layer(): lax.ppermute(inner_act, 'fsdp', ring_pairs(fsdp_count, shift))  21.2 us
    dot_general x4, matrix products, gate_and_up(): jnp.einsum('jrd,jdh->jrh', rows_in, gate_w, preferred_element_type=jnp.fl...  16.2 us
    dot_general x4, matrix products, gate_and_up(): jnp.einsum('jrd,jdh->jrh', rows_in, up_w, preferred_element_type=jnp.floa...  13.5 us
    ppermute x3, waiting for transfers between devices, other_half(): return lax.ppermute(value, 'zhalf', [(0, 1), (1, 0)])  13.3 us
  transfers between devices with their start and end apart: 18, of which 11 were waited for; matrix products, arithmetic and copies ran while one was open for 8% of the time, Pallas kernels for 0%

commit v1 on v0

--- a/solution.py
+++ b/solution.py
@@ -94,7 +94,15 @@
         .astype(jnp.bfloat16)
         .reshape(fsdp_count * inner_devices, local_experts, halves * capacity, chunk)
     )
-    arrived = lax.all_to_all(outgoing, ("fsdp", "inner"), 0, 2, tiled=True)
+    arrived = jnp.concatenate(
+        lax.all_to_all(
+            jnp.stack(jnp.split(outgoing, lax.axis_size(("fsdp", "inner")), axis=0)),
+            ("fsdp", "inner"),
+            0,
+            0,
+        ),
+        axis=2,
+    )
     sources = fsdp_count * inner_devices * halves
     arrived_blocks = arrived.reshape(local_experts, fsdp_count, -1, chunk)
 

time: 330 us -> 343 us (1.039); the launches traced: 329 us -> 338 us
  local copies, waits for them, and re-layouts: 16.9 us -> 23.4 us
    ppermute x3, waiting for transfers between devices: 13.3 us -> 20.6 us  [other_half(): return lax.ppermute(value, 'zhalf', [(0, 1), (1, 0)])]
    unnamed x27 -> x41, local copies, waits for them, and re-layouts: 0.87 us -> 7.66 us
    ppermute x1, waiting for transfers between devices: 5.71 us -> 0.36 us  [body(): lax.ppermute(own_routes, ('section', 'zhalf'), [(0, 3), (3, 0), (1, 2), (...]
    ppermute x3, starting transfers between devices: 9 us -> 4.61 us  [other_half(): return lax.ppermute(value, 'zhalf', [(0, 1), (1, 0)])]
    ppermute x1, starting transfers between devices: 0.01 us -> 3.69 us  [body(): lax.ppermute(own_routes, ('section', 'zhalf'), [(0, 3), (3, 0), (1, 2), (...]
  transfers between devices with their start and end apart: 18 -> 18, of which waited for: 11 -> 12; matrix products, arithmetic and copies ran while one was open for 8% -> 9% of each run, Pallas kernels for 0% -> 0%
where the time goes in v1:
time: 343 us; the launch traced here: 338 us
  waiting for transfers between devices  200 us (58%)
  matrix products  47.5 us (14%)
  starting transfers between devices  29.2 us (9%)
  blocking collectives  28.2 us (8%)
  local copies, waits for them, and re-layouts  23.4 us (7%)
  other arithmetic  7.5 us (2%)
    all_to_all x2, waiting for transfers between devices, expert_layer(): lax.all_to_all(sending.reshape(sources, group_slots, chunk), ('fsdp', 'zh...  66.3 us
    ppermute x2, waiting for transfers between devices, expert_layer(): lax.ppermute(outgoing_pair, 'fsdp', ring_pairs(fsdp_count, shift))  56.9 us
    all_to_all x1, blocking collectives, expert_layer(): lax.all_to_all(jnp.stack(jnp.split(outgoing, lax.axis_size(('fsdp', 'inne...  28.2 us
    all_to_all x1, waiting for transfers between devices, expert_layer(): lax.all_to_all(jnp.stack(jnp.split(outgoing, lax.axis_size(('fsdp', 'inne...  27.8 us
    ppermute x2, waiting for transfers between devices, expert_layer(): lax.ppermute(inner_act, 'fsdp', ring_pairs(fsdp_count, shift))  21.5 us
    ppermute x3, waiting for transfers between devices, other_half(): return lax.ppermute(value, 'zhalf', [(0, 1), (1, 0)])  20.6 us
    dot_general x4, matrix products, gate_and_up(): jnp.einsum('jrd,jdh->jrh', rows_in, up_w, preferred_element_type=jnp.floa...  16.8 us
    dot_general x4, matrix products, gate_and_up(): jnp.einsum('jrd,jdh->jrh', rows_in, gate_w, preferred_element_type=jnp.fl...  13.2 us
  transfers between devices with their start and end apart: 18, of which 12 were waited for; matrix products, arithmetic and copies ran while one was open for 9% of the time, Pallas kernels for 0%

profile of v1, /device:TPU:0, one launch (start us, length us, event | category | flops | bytes accessed | tf_op | source)
XLA Modules:
  0.0 337.8 jit_solution(2989197542513364269)
XLA Ops:
  0.6 0.8 copy.121
  1.4 0.6 collective-permute-start
  2.0 3.7 %collective-permute-start.5 = (s32[128,6]{1,0:T(8,128)S(1)}, s32[128,6]{1,0:T(8,128)S(1)}, u32[]{:S(2)}, u32[]{:S(2)}) collective-permute-start(s32[128,6]{1,0:T(8,128)S(1)} %bitcast.284), channel_id=1, source_target_pairs={{0,20},{20,0},{4,16},{16,4},{1,21},{21,1},{5,17},{17,5},{2,22},{22... | collective-permute-start | bytes 9224 | tf_op jit(solution)/shard_map/ppermute | solution.py:171
  5.7 0.9 bitcast_convert_fusion
  6.6 0.7 pad_maximum_fusion.4
  7.9 1.1 fusion.78
  9.5 2.6 collective-permute-start.3
  15.3 9.2 %collective-permute-done.3 = bf16[64,2048]{1,0:T(8,128)(2,1)S(1)} collective-permute-done((bf16[64,2048]{1,0:T(8,128)(2,1)S(1)}, bf16[64,2048]{1,0:T(8,128)(2,1)S(1)}, u32[]{:S(2)}, u32[]{:S(2)}) %collective-permute-start.3) | collective-permute-done | bytes 262176 | tf_op jit(solution)/shard_map/ppermute | solution.py:49
  24.7 0.7 copy-done.2
  26.1 0.7 convert_bitcast_fusion.3
  26.8 1.6 copy.128
  28.4 0.8 fusion.104
  29.2 0.8 fusion.103
  29.9 0.8 fusion.102
  30.7 0.8 fusion.101
  31.5 0.8 fusion.100
  32.2 0.8 fusion.99
  33.0 0.8 fusion.98
  33.8 0.8 fusion.97
  34.5 4.0 %all-to-all-start = ((bf16[8,1,4,28,1024]{4,2,3,1,0:T(4,128)(2,1)}), bf16[8,1,4,28,1024]{4,2,3,1,0:T(4,128)(2,1)S(1)}, u32[]{:S(2)}, u32[]{:S(2)}) async-start(bf16[8,1,4,28,1024]{4,2,3,1,0:T(4,128)(2,1)} %fusion.97), calls=%async_computation | async-start | bytes 3670016 | tf_op jit(solution)/shard_map/all_to_all | solution.py:98
  38.6 27.8 %all-to-all-done = bf16[8,1,4,28,1024]{4,2,3,1,0:T(4,128)(2,1)S(1)} async-done(((bf16[8,1,4,28,1024]{4,2,3,1,0:T(4,128)(2,1)}), bf16[8,1,4,28,1024]{4,2,3,1,0:T(4,128)(2,1)S(1)}, u32[]{:S(2)}, u32[]{:S(2)}) %all-to-all-start) | async-done | bytes 1835040 | tf_op jit(solution)/shard_map/all_to_all | solution.py:98
  66.4 0.6 constant_dynamic-slice_fusion.4
  67.0 4.8 %fusion.33 = bf16[1,4,112,768]{3,2,1,0:T(8,128)(2,1)S(1)} fusion(bf16[4,1024,768]{2,1,0:T(8,128)(2,1)} %collective-permute-done.7, pred[]{:T(512)S(6)} %eq.78, bf16[4,1,112,1024]{3,0,2,1:T(4,128)(2,1)S(1)} %get-tuple-element.19, bf16[1,4,1024,768]{3,2,1,0:T(8,128)(2,1)} %param.13), kind=kOutput, calls=%fused_computation.49 | convolution fusion | flops 708132864 | bytes 14188545 | tf_op jit(solution)/shard_map/jrd,jdh->jrh/dot_general | solution.py:111
  71.9 1.8 fusion.32
  73.9 0.6 collective-permute-start.8
  74.5 30.5 %collective-permute-done.8 = bf16[2,4,112,768]{3,2,1,0:T(8,128)(2,1)S(1)} collective-permute-done((bf16[2,4,112,768]{3,2,1,0:T(8,128)(2,1)S(1)}, bf16[2,4,112,768]{3,2,1,0:T(8,128)(2,1)S(1)}, u32[]{:S(2)}, u32[]{:S(2)}) %collective-permute-start.8) | collective-permute-done | bytes 1376288 | tf_op jit(solution)/shard_map/ppermute | solution.py:120
  105.0 1.9 fusion.27
  106.9 2.0 multiply_convert_fusion.1
  109.0 0.6 collective-permute-start.9
  109.6 11.2 %collective-permute-done.9 = bf16[4,112,768]{2,1,0:T(8,128)(2,1)S(1)} collective-permute-done((bf16[4,112,768]{2,1,0:T(8,128)(2,1)S(1)}, bf16[4,112,768]{2,1,0:T(8,128)(2,1)S(1)}, u32[]{:S(2)}, u32[]{:S(2)}) %collective-permute-start.9) | collective-permute-done | bytes 688160 | tf_op jit(solution)/shard_map/ppermute | solution.py:130
  120.9 0.6 gather_fusion
  121.7 0.7 copy.131
  122.5 4.7 %convert_bitcast_fusion.2 = bf16[2,2,4,4,14,1024]{5,4,1,2,0,3:T(8,128)(2,1)S(1)} fusion(bf16[4,768,1024]{2,1,0:T(8,128)(2,1)} %collective-permute-done.2, pred[]{:T(512)S(6)} %eq.78, bf16[2,4,4,2,14,768]{5,1,4,3,2,0:T(4,128)(2,1)S(1)} %bitcast.277, bf16[1,4,768,1024]{3,2,1,0:T(8,128)(2,1)} %param.14), kind=kOutput, calls=%fused_computation.28 | convolution fusion | flops 1413349376 | bytes 15794177 | tf_op jit(solution)/shard_map/fjipch,jhd->fpijcd/dot_general | solution.py:135
  127.4 1.5 reshape.226
  128.9 5.4 %all-to-all-start.1 = ((bf16[16,56,1024]{2,1,0:T(8,128)(2,1)}), bf16[16,56,1024]{2,1,0:T(8,128)(2,1)S(1)}, u32[]{:S(2)}, u32[]{:S(2)}) async-start(bf16[16,56,1024]{2,1,0:T(8,128)(2,1)} %reshape.226), calls=%async_computation.1 | async-start | bytes 3670016 | tf_op jit(solution)/shard_map/all_to_all | solution.py:138
  135.0 39.0 %all-to-all-done.1 = bf16[16,56,1024]{2,1,0:T(8,128)(2,1)S(1)} async-done(((bf16[16,56,1024]{2,1,0:T(8,128)(2,1)}), bf16[16,56,1024]{2,1,0:T(8,128)(2,1)S(1)}, u32[]{:S(2)}, u32[]{:S(2)}) %all-to-all-start.1) | async-done | bytes 1835040 | tf_op jit(solution)/shard_map/all_to_all | solution.py:138
  174.1 1.7 fusion.70
  175.8 2.0 collective-permute-start.10
  178.0 10.9 %collective-permute-done.10 = bf16[64,2048]{1,0:T(8,128)(2,1)S(1)} collective-permute-done((bf16[64,2048]{1,0:T(8,128)(2,1)S(1)}, bf16[64,2048]{1,0:T(8,128)(2,1)S(1)}, u32[]{:S(2)}, u32[]{:S(2)}) %collective-permute-start.10) | collective-permute-done | bytes 262176 | tf_op jit(solution)/shard_map/ppermute | solution.py:49
  189.8 0.7 convert_bitcast_fusion.1
  190.5 1.6 copy.142
  192.9 28.2 %all_to_all.26 = bf16[8,1,4,28,1024]{4,2,3,1,0:T(4,128)(2,1)S(1)} all-to-all(bf16[8,1,4,28,1024]{4,2,3,1,0:T(4,128)(2,1)S(1)} %fusion.89), channel_id=1, replica_groups=mesh['section'=2,'fsdp'=2,'zhalf'=2,'inner'=4] {'fsdp','inner'}, dimensions={0} | all-to-all | bytes 3670016 | tf_op jit(solution)/shard_map/all_to_all | solution.py:98
  221.1 0.6 constant_dynamic-slice_fusion.2
  221.8 5.1 %fusion.35 = bf16[1,4,112,768]{3,2,1,0:T(8,128)(2,1)S(1)} fusion(bf16[4,1024,768]{2,1,0:T(8,128)(2,1)} %collective-permute-done.7, pred[]{:T(512)S(6)} %eq.172, bf16[4,1,112,1024]{3,0,2,1:T(4,128)(2,1)S(1)} %get-tuple-element.17, bf16[1,4,1024,768]{3,2,1,0:T(8,128)(2,1)S(1)} %bitcast.301), kind=kOutput, calls=%fused_computation.51 | convolution fusion | flops 708132864 | bytes 14188545 | tf_op jit(solution)/shard_map/jrd,jdh->jrh/dot_general | solution.py:111
  226.9 4.7 %fusion.34 = bf16[1,4,112,768]{3,2,1,0:T(8,128)(2,1)S(1)} fusion(bf16[4,1024,768]{2,1,0:T(8,128)(2,1)} %collective-permute-done.6, pred[]{:T(512)S(6)} %eq.172, bf16[4,1,112,1024]{3,0,2,1:T(4,128)(2,1)S(1)} %get-tuple-element.17, bf16[1,4,1024,768]{3,2,1,0:T(8,128)(2,1)S(1)} %bitcast.296), kind=kOutput, calls=%fused_computation.50 | convolution fusion | flops 708132864 | bytes 14188545 | tf_op jit(solution)/shard_map/jrd,jdh->jrh/dot_general | solution.py:110
  231.8 0.6 collective-permute-start.11
  232.4 26.4 %collective-permute-done.11 = bf16[2,4,112,768]{3,2,1,0:T(8,128)(2,1)S(1)} collective-permute-done((bf16[2,4,112,768]{3,2,1,0:T(8,128)(2,1)S(1)}, bf16[2,4,112,768]{3,2,1,0:T(8,128)(2,1)S(1)}, u32[]{:S(2)}, u32[]{:S(2)}) %collective-permute-start.11) | collective-permute-done | bytes 1376288 | tf_op jit(solution)/shard_map/ppermute | solution.py:120
  258.8 4.7 %fusion.25 = f32[4,112,768]{2,1,0:T(8,128)S(1)} fusion(bf16[4,1024,768]{2,1,0:T(8,128)(2,1)} %collective-permute-done.6, pred[]{:T(512)S(6)} %eq.172, bf16[4,1,112,1024]{3,0,2,1:T(4,128)(2,1)S(1)} %get-tuple-element.18, bf16[2,4,112,768]{3,2,1,0:T(8,128)(2,1)S(1)} %collective-permute-done.11, bf16[1,4,1024,768]{3,2,1,0:T(8,128)(2,1)S(1)} %bitcast.296), kind=kOutput, calls=%fused_computation.33 | convolution fusion | flops 708476928 | bytes 15564801 | tf_op jit(solution)/shard_map/jrd,jdh->jrh/dot_general | solution.py:110
  263.5 4.9 %multiply_convert_fusion = bf16[4,112,768]{2,1,0:T(8,128)(2,1)S(1)} fusion(f32[4,112,768]{2,1,0:T(8,128)S(1)} %fusion.25, bf16[4,1024,768]{2,1,0:T(8,128)(2,1)} %collective-permute-done.7, pred[]{:T(512)S(6)} %eq.172, bf16[4,1,112,1024]{3,0,2,1:T(4,128)(2,1)S(1)} %get-tuple-element.18, bf16[2,4,112,768]{3,2,1,0:T(8,128)(2,1)S(1)} %collective-permute-done.11, ...), kind=kOutput, calls=%fused_computation.40 | convolution fusion | flops 710541312 | bytes 16252929 | tf_op jit(solution)/shard_map/jrd,jdh->jrh/dot_general | solution.py:111
  268.5 0.6 collective-permute-start.12
  269.1 10.4 %collective-permute-done.12 = bf16[4,112,768]{2,1,0:T(8,128)(2,1)S(1)} collective-permute-done((bf16[4,112,768]{2,1,0:T(8,128)(2,1)S(1)}, bf16[4,112,768]{2,1,0:T(8,128)(2,1)S(1)}, u32[]{:S(2)}, u32[]{:S(2)}) %collective-permute-start.12) | collective-permute-done | bytes 688160 | tf_op jit(solution)/shard_map/ppermute | solution.py:130
  279.6 0.6 gather_fusion.1
  280.5 0.7 copy.145
  281.2 6.5 %convert_bitcast_fusion = bf16[2,2,4,4,14,1024]{5,4,1,2,0,3:T(8,128)(2,1)S(1)} fusion(bf16[4,768,1024]{2,1,0:T(8,128)(2,1)} %collective-permute-done.2, pred[]{:T(512)S(6)} %eq.172, bf16[2,4,4,2,14,768]{5,1,4,3,2,0:T(4,128)(2,1)S(1)} %bitcast.278, bf16[1,4,768,1024]{3,2,1,0:T(8,128)(2,1)} %param.14), kind=kOutput, calls=%fused_computation.26 | convolution fusion | flops 1413349376 | bytes 15794177 | tf_op jit(solution)/shard_map/fjipch,jhd->fpijcd/dot_general | solution.py:135
  287.9 1.5 reshape.228
  289.4 4.5 %all-to-all-start.3 = ((bf16[16,56,1024]{2,1,0:T(8,128)(2,1)}), bf16[16,56,1024]{2,1,0:T(8,128)(2,1)S(1)}, u32[]{:S(2)}, u32[]{:S(2)}) async-start(bf16[16,56,1024]{2,1,0:T(8,128)(2,1)} %reshape.228), calls=%async_computation.3 | async-start | bytes 3670016 | tf_op jit(solution)/shard_map/all_to_all | solution.py:138
  294.6 27.4 %all-to-all-done.3 = bf16[16,56,1024]{2,1,0:T(8,128)(2,1)S(1)} async-done(((bf16[16,56,1024]{2,1,0:T(8,128)(2,1)}), bf16[16,56,1024]{2,1,0:T(8,128)(2,1)S(1)}, u32[]{:S(2)}, u32[]{:S(2)}) %all-to-all-start.3) | async-done | bytes 1835040 | tf_op jit(solution)/shard_map/all_to_all | solution.py:138
  322.2 1.7 multiply_reduce_fusion
  323.9 1.4 pad_maximum_fusion.5
  325.2 0.6 broadcast_in_dim.32
  325.8 3.1 all-to-all-start.4
  329.3 6.7 %all-to-all-done.4 = f32[32,1,2]{2,1,0:T(1,128)S(1)} async-done(((f32[32,1,2]{2,1,0:T(1,128)}), f32[32,1,2]{2,1,0:T(1,128)S(1)}, u32[]{:S(2)}, u32[]{:S(2)}) %all-to-all-start.4) | async-done | bytes 288 | tf_op jit(solution)/shard_map/all_to_all | solution.py:193
  336.1 0.6 dynamic_slice.48
  336.7 0.8 maximum_select_fusion
  (123 shorter events, 10.4 us)
Async XLA Ops:
  1.4 11.6 %collective-permute-start = (s32[128,6]{1,0:T(8,128)S(1)}, s32[128,6]{1,0:T(8,128)S(1)}, u32[]{:S(2)}, u32[]{:S(2)}) collective-permute-start(s32[128,6]{1,0:T(8,128)S(1)} %bitcast.283), channel_id=1, source_target_pairs={{0,16},{16,0},{1,17},{17,1},{2,18},{18,2},{3,19},{19,3},{4,20},{20... | collective-permute-start | bytes 9224 | tf_op jit(solution)/shard_map/ppermute | solution.py:12
  2.0 7.5 %collective-permute-start.5 = (s32[128,6]{1,0:T(8,128)S(1)}, s32[128,6]{1,0:T(8,128)S(1)}, u32[]{:S(2)}, u32[]{:S(2)}) collective-permute-start(s32[128,6]{1,0:T(8,128)S(1)} %bitcast.284), channel_id=1, source_target_pairs={{0,20},{20,0},{4,16},{16,4},{1,21},{21,1},{5,17},{17,5},{2,22},{22... | collective-permute-start | bytes 9224 | tf_op jit(solution)/shard_map/ppermute | solution.py:171
  5.7 6.9 %collective-permute-start.4 = (s32[128,6]{1,0:T(8,128)S(1)}, s32[128,6]{1,0:T(8,128)S(1)}, u32[]{:S(2)}, u32[]{:S(2)}) collective-permute-start(s32[128,6]{1,0:T(8,128)S(1)} %bitcast.285), channel_id=1, source_target_pairs={{0,4},{4,0},{1,5},{5,1},{2,6},{6,2},{3,7},{7,3},{8,12},{12,8},{9,1... | collective-permute-start | bytes 9224 | tf_op jit(solution)/shard_map/ppermute | solution.py:49
  7.4 17.3 %copy-start.1 = (f32[1,2048]{1,0:T(1,128)S(1)}, f32[1,2048]{1,0:T(1,128)}, u32[]{:S(2)}) copy-start(f32[1,2048]{1,0:T(1,128)} %param.10) | copy-start | bytes 24580
  7.4 17.3 %collective-permute-start.1 = (f32[2048,33]{0,1:T(8,128)S(1)}, f32[2048,33]{0,1:T(8,128)S(1)}, u32[]{:S(2)}, u32[]{:S(2)}) collective-permute-start(f32[2048,33]{0,1:T(8,128)S(1)} %pad_maximum_fusion.4), channel_id=1, source_target_pairs={{0,16},{16,0},{1,17},{17,1},{2,18},{18,2},{3,19},{19,3},{4,20},{20... | collective-permute-start | bytes 811016 | tf_op jit(solution)/shard_map/ppermute | solution.py:12
  7.5 64.3 %collective-permute-start.6 = (bf16[4,1024,768]{2,1,0:T(8,128)(2,1)}, bf16[4,1024,768]{2,1,0:T(8,128)(2,1)}, u32[]{:S(2)}, u32[]{:S(2)}) collective-permute-start(bf16[4,1024,768]{2,1,0:T(8,128)(2,1)} %bitcast.292), channel_id=1, source_target_pairs={{0,16},{16,0},{1,17},{17,1},{2,18},{18,2},{3,19},{19,3},{4,20},{20... | collective-permute-start | bytes 18874376 | tf_op jit(solution)/shard_map/ppermute | solution.py:12
  9.5 15.1 %collective-permute-start.3 = (bf16[64,2048]{1,0:T(8,128)(2,1)S(1)}, bf16[64,2048]{1,0:T(8,128)(2,1)S(1)}, u32[]{:S(2)}, u32[]{:S(2)}) collective-permute-start(bf16[64,2048]{1,0:T(8,128)(2,1)S(1)} %get-tuple-element.16), channel_id=1, source_target_pairs={{0,4},{4,0},{1,5},{5,1},{2,6},{6,2},{3,7},{7,3},{8,12},{12,8},{9,1... | collective-permute-start | bytes 786440 | tf_op jit(solution)/shard_map/ppermute | solution.py:49
  12.5 54.5 %collective-permute-start.7 = (bf16[4,1024,768]{2,1,0:T(8,128)(2,1)}, bf16[4,1024,768]{2,1,0:T(8,128)(2,1)}, u32[]{:S(2)}, u32[]{:S(2)}) collective-permute-start(bf16[4,1024,768]{2,1,0:T(8,128)(2,1)} %bitcast.297), channel_id=1, source_target_pairs={{0,16},{16,0},{1,17},{17,1},{2,18},{18,2},{3,19},{19,3},{4,20},{20... | collective-permute-start | bytes 18874376 | tf_op jit(solution)/shard_map/ppermute | solution.py:12
  24.7 0.7 copy-start.2
  34.5 31.8 %all-to-all-start = ((bf16[8,1,4,28,1024]{4,2,3,1,0:T(4,128)(2,1)}), bf16[8,1,4,28,1024]{4,2,3,1,0:T(4,128)(2,1)S(1)}, u32[]{:S(2)}, u32[]{:S(2)}) async-start(bf16[8,1,4,28,1024]{4,2,3,1,0:T(4,128)(2,1)} %fusion.97), calls=%async_computation | async-start | bytes 3670016 | tf_op jit(solution)/shard_map/all_to_all | solution.py:98
  38.5 83.9 %collective-permute-start.2 = (bf16[4,768,1024]{2,1,0:T(8,128)(2,1)}, bf16[4,768,1024]{2,1,0:T(8,128)(2,1)}, u32[]{:S(2)}, u32[]{:S(2)}) collective-permute-start(bf16[4,768,1024]{2,1,0:T(8,128)(2,1)} %bitcast.302), channel_id=1, source_target_pairs={{0,16},{16,0},{1,17},{17,1},{2,18},{18,2},{3,19},{19,3},{4,20},{20... | collective-permute-start | bytes 18874376 | tf_op jit(solution)/shard_map/ppermute | solution.py:12
  66.4 5.5 %slice-start = ((s8[6291456]{0:T(1024)(128)(4,1)}), s8[4194304]{0:T(1024)(128)(4,1)S(1)}, s32[]{:S(2)}) async-start(s8[6291456]{0:T(1024)(128)(4,1)} %bitcast.293), calls=%async_computation.5 | async-start | bytes 8388608
  67.0 4.8 %slice-start.1 = ((s8[6291456]{0:T(1024)(128)(4,1)}), s8[2097152]{0:T(1024)(128)(4,1)S(1)}, s32[]{:S(2)}) async-start(s8[6291456]{0:T(1024)(128)(4,1)} %bitcast.293), calls=%async_computation.6 | async-start | bytes 4194304
  73.7 33.2 %slice-start.4 = ((s8[6291456]{0:T(1024)(128)(4,1)}), s8[4194304]{0:T(1024)(128)(4,1)S(1)}, s32[]{:S(2)}) async-start(s8[6291456]{0:T(1024)(128)(4,1)} %bitcast.298), calls=%async_computation.9 | async-start | bytes 8388608
  73.9 31.1 %collective-permute-start.8 = (bf16[2,4,112,768]{3,2,1,0:T(8,128)(2,1)S(1)}, bf16[2,4,112,768]{3,2,1,0:T(8,128)(2,1)S(1)}, u32[]{:S(2)}, u32[]{:S(2)}) collective-permute-start(bf16[2,4,112,768]{3,2,1,0:T(8,128)(2,1)S(1)} %pad_maximum_fusion), channel_id=1, source_target_pairs={{0,8},{8,0},{1,9},{9,1},{2,10},{10,2},{3,11},{11,3},{4,12},{12,4},... | collective-permute-start | bytes 4128776 | tf_op jit(solution)/shard_map/ppermute | solution.py:120
  105.0 1.9 slice-start.5
  109.0 11.8 %collective-permute-start.9 = (bf16[4,112,768]{2,1,0:T(8,128)(2,1)S(1)}, bf16[4,112,768]{2,1,0:T(8,128)(2,1)S(1)}, u32[]{:S(2)}, u32[]{:S(2)}) collective-permute-start(bf16[4,112,768]{2,1,0:T(8,128)(2,1)S(1)} %multiply_convert_fusion.1), channel_id=1, source_target_pairs={{0,8},{8,0},{1,9},{9,1},{2,10},{10,2},{3,11},{11,3},{4,12},{12,4},... | collective-permute-start | bytes 2064392 | tf_op jit(solution)/shard_map/ppermute | solution.py:130
  128.9 5.5 %copy-start = (bf16[1,2048,32]{1,2,0:T(8,128)(2,1)S(1)}, bf16[1,2048,32]{1,2,0:T(8,128)(2,1)}, u32[]{:S(2)}) copy-start(bf16[1,2048,32]{1,2,0:T(8,128)(2,1)} %param.11) | copy-start | bytes 393220
  128.9 5.5 %copy-start.3 = (f32[2048,33]{0,1:T(8,128)S(1)}, f32[2048,33]{0,1:T(8,128)}, u32[]{:S(2)}) copy-start(f32[2048,33]{0,1:T(8,128)} %copy-done.2) | copy-start | bytes 811012
  128.9 45.1 %all-to-all-start.1 = ((bf16[16,56,1024]{2,1,0:T(8,128)(2,1)}), bf16[16,56,1024]{2,1,0:T(8,128)(2,1)S(1)}, u32[]{:S(2)}, u32[]{:S(2)}) async-start(bf16[16,56,1024]{2,1,0:T(8,128)(2,1)} %reshape.226), calls=%async_computation.1 | async-start | bytes 3670016 | tf_op jit(solution)/shard_map/all_to_all | solution.py:138
  175.8 13.1 %collective-permute-start.10 = (bf16[64,2048]{1,0:T(8,128)(2,1)S(1)}, bf16[64,2048]{1,0:T(8,128)(2,1)S(1)}, u32[]{:S(2)}, u32[]{:S(2)}) collective-permute-start(bf16[64,2048]{1,0:T(8,128)(2,1)S(1)} %get-tuple-element.33), channel_id=1, source_target_pairs={{0,4},{4,0},{1,5},{5,1},{2,6},{6,2},{3,7},{7,3},{8,12},{12,8},{9,1... | collective-permute-start | bytes 786440 | tf_op jit(solution)/shard_map/ppermute | solution.py:49
  190.5 31.2 %slice-start.6 = ((s8[6291456]{0:T(1024)(128)(4,1)}), s8[4194304]{0:T(1024)(128)(4,1)S(1)}, s32[]{:S(2)}) async-start(s8[6291456]{0:T(1024)(128)(4,1)} %bitcast.300), calls=%async_computation.11 | async-start | bytes 8388608
  192.8 29.0 %slice-start.7 = ((s8[6291456]{0:T(1024)(128)(4,1)}), s8[2097152]{0:T(1024)(128)(4,1)S(1)}, s32[]{:S(2)}) async-start(s8[6291456]{0:T(1024)(128)(4,1)} %bitcast.300), calls=%async_computation.12 | async-start | bytes 4194304
  221.1 5.8 %slice-start.2 = ((s8[6291456]{0:T(1024)(128)(4,1)}), s8[4194304]{0:T(1024)(128)(4,1)S(1)}, s32[]{:S(2)}) async-start(s8[6291456]{0:T(1024)(128)(4,1)} %bitcast.295), calls=%async_computation.7 | async-start | bytes 8388608
  221.8 5.1 %slice-start.3 = ((s8[6291456]{0:T(1024)(128)(4,1)}), s8[2097152]{0:T(1024)(128)(4,1)S(1)}, s32[]{:S(2)}) async-start(s8[6291456]{0:T(1024)(128)(4,1)} %bitcast.295), calls=%async_computation.8 | async-start | bytes 4194304
  231.8 27.0 %collective-permute-start.11 = (bf16[2,4,112,768]{3,2,1,0:T(8,128)(2,1)S(1)}, bf16[2,4,112,768]{3,2,1,0:T(8,128)(2,1)S(1)}, u32[]{:S(2)}, u32[]{:S(2)}) collective-permute-start(bf16[2,4,112,768]{3,2,1,0:T(8,128)(2,1)S(1)} %pad_maximum_fusion.2), channel_id=1, source_target_pairs={{0,8},{8,0},{1,9},{9,1},{2,10},{10,2},{3,11},{11,3},{4,12},{12,4},... | collective-permute-start | bytes 4128776 | tf_op jit(solution)/shard_map/ppermute | solution.py:120
  268.5 11.0 %collective-permute-start.12 = (bf16[4,112,768]{2,1,0:T(8,128)(2,1)S(1)}, bf16[4,112,768]{2,1,0:T(8,128)(2,1)S(1)}, u32[]{:S(2)}, u32[]{:S(2)}) collective-permute-start(bf16[4,112,768]{2,1,0:T(8,128)(2,1)S(1)} %multiply_convert_fusion), channel_id=1, source_target_pairs={{0,8},{8,0},{1,9},{9,1},{2,10},{10,2},{3,11},{11,3},{4,12},{12,4},... | collective-permute-start | bytes 2064392 | tf_op jit(solution)/shard_map/ppermute | solution.py:130
  289.4 4.6 %copy-start.4 = (f32[2048,33]{0,1:T(8,128)S(1)}, f32[2048,33]{0,1:T(8,128)}, u32[]{:S(2)}) copy-start(f32[2048,33]{0,1:T(8,128)} %copy-done.2) | copy-start | bytes 811012
  289.4 32.6 %all-to-all-start.3 = ((bf16[16,56,1024]{2,1,0:T(8,128)(2,1)}), bf16[16,56,1024]{2,1,0:T(8,128)(2,1)S(1)}, u32[]{:S(2)}, u32[]{:S(2)}) async-start(bf16[16,56,1024]{2,1,0:T(8,128)(2,1)} %reshape.228), calls=%async_computation.3 | async-start | bytes 3670016 | tf_op jit(solution)/shard_map/all_to_all | solution.py:138
  325.8 10.2 %all-to-all-start.4 = ((f32[32,1,2]{2,1,0:T(1,128)}), f32[32,1,2]{2,1,0:T(1,128)S(1)}, u32[]{:S(2)}, u32[]{:S(2)}) async-start(f32[32,1,2]{2,1,0:T(1,128)} %broadcast_in_dim.32), calls=%async_computation.4 | async-start | bytes 32768 | tf_op jit(solution)/shard_map/all_to_all | solution.py:193
  329.0 7.7 %collective-permute-start.13 = (bf16[64,1024]{1,0:T(8,128)(2,1)S(1)}, bf16[64,1024]{1,0:T(8,128)(2,1)S(1)}, u32[]{:S(2)}, u32[]{:S(2)}) collective-permute-start(bf16[64,1024]{1,0:T(8,128)(2,1)S(1)} %get-tuple-element.28), channel_id=1, source_target_pairs={{0,16},{16,0},{1,17},{17,1},{2,18},{18,2},{3,19},{19,3},{4,20},{20... | collective-permute-start | bytes 393224 | tf_op jit(solution)/shard_map/ppermute | solution.py:12
